TPU v7x, 512 devices: a whole 4x8x8 slice. The times are simulated.
512 devices in a mesh: series: 8 (over y_hi, x), tm: 64 (over z, y_lo, core).
Axes of the slice: x: 4, y: 8 (y_hi: 2, y_lo: 4; y = y_hi * 4 + y_lo), z: 8, core: 2. Of those that a mesh axis runs over, the one named last changes fastest.
Arguments:
- y_obs: bfloat16 [32768, 32768], P('series', 'tm'), may hold values from -6 to 6
- tile_mask: int32 [256, 256], P('series', 'tm'), may hold values 0 or 1
- factors: float32 [32768, 128], P(('series', 'tm')), may hold values from -0.5 to 0.5
- adam_m: float32 [32768, 128], P(('series', 'tm')), may hold values from -3 to 3
- adam_v: float32 [32768, 128], P(('series', 'tm')), may hold values from 0.1 to 10
- basis: float32 [128, 32768], P('series', 'tm'), may hold values from -6 to 6
- dilations: int32 [4], replicated, may hold values from 1 to 32, as said below
- conv_w: bfloat16 [4, 2, 128, 128], replicated, may hold values from -0.375 to 0.375
- conv_b: float32 [4, 128], replicated, may hold values from -3 to 3
Outputs:
- factors_new: float32 [32768, 128], P(('series', 'tm'))
- m_new: float32 [32768, 128], P(('series', 'tm'))
- v_new: float32 [32768, 128], P(('series', 'tm'))
- basis_new: float32 [128, 32768], P('series', 'tm')
Inputs may be any that keep to these rules, and one draw needn't show every extreme that they name: `dilations`: at least one layer has dilation 32.
All inputs are finite; a program needn't handle non-finite values. No bound on the sum of `tile_mask` on one device may be relied on, other than what follows from the above.
Results may differ from a plain program's by a relative error of at most 0.0031.
Values may be sent and summed in bfloat16 or wider, within the bound.
No kernel may reach another device: no remote copies, remote signals or barrier semaphores. Data moves between devices by JAX's collectives and lax.ppermute only.
A program may use at most 64 MiB of HBM per device.

v0:
```python
import math
import jax
import jax.numpy as jnp
from jax import lax
from jax.sharding import PartitionSpec as P

K = 128
TILE = 128
LAYERS = 4
D_MAX = 32


def passed_along(value, axis, steps):
    count = lax.axis_size(axis)
    leading, last = (max(0, -steps), min(count, count - steps))
    return lax.ppermute(value, axis, [(source, source + steps) for source in range(leading, last)])


def expand(tiles, tile):
    rows, cols = tiles.shape
    ones = tiles.astype(jnp.float32)
    return jnp.broadcast_to(ones[:, None, :, None], (rows, tile, cols, tile)).reshape(
        rows * tile, cols * tile
    )


def adam_update(factors, adam_m, adam_v, grad_f):
    m_new = 0.9 * adam_m + 0.1 * grad_f
    v_new = 0.999 * adam_v + 0.001 * grad_f * grad_f
    m_hat = m_new / (1.0 - 0.9**10)
    v_hat = v_new / (1.0 - 0.999**10)
    return (factors - 0.01 * m_hat / (jnp.sqrt(v_hat) + 1e-08), m_new, v_new)


def conv_layer(hidden, hb, past, weights, biases):
    z_val = jnp.dot(weights[0], past, preferred_element_type=jnp.float32)
    z_val = z_val + jnp.dot(weights[1], hb, preferred_element_type=jnp.float32)
    z_val = z_val + biases[:, None]
    return hidden + jax.nn.relu(z_val)


def on_device(y_obs, tile_mask, factors, adam_m, adam_v, basis, dilations, conv_w, conv_b):
    own_rows = factors.shape[0]
    width = basis.shape[1]
    rank_part = basis.shape[0]
    total_time = width * lax.axis_size("tm")
    total_series = own_rows * lax.axis_size("tm") * lax.axis_size("series")
    f_block = lax.all_gather(factors.astype(jnp.bfloat16), "tm", axis=0, tiled=True)
    x_full = lax.all_gather(basis.astype(jnp.bfloat16), "series", axis=0, tiled=True)
    pred = jnp.dot(f_block, x_full, preferred_element_type=jnp.float32)
    resid = expand(tile_mask, TILE) * (y_obs.astype(jnp.float32) - pred)
    rb = resid.astype(jnp.bfloat16)
    scale_f = 1.0 / math.sqrt(total_time)
    contract_time = (((1,), (1,)), ((), ()))
    grad_f = lax.psum_scatter(
        -lax.dot_general(rb, x_full, contract_time, preferred_element_type=jnp.float32) * scale_f,
        "tm",
        scatter_dimension=0,
        tiled=True,
    )
    factors_new, m_new, v_new = adam_update(factors, adam_m, adam_v, grad_f)
    partial_x = -lax.dot_general(
        f_block, rb, (((0,), (0,)), ((), ())), preferred_element_type=jnp.float32
    )
    partial_x = partial_x * math.sqrt(K / total_series)
    grad_x = lax.psum_scatter(partial_x, "series", scatter_dimension=0, tiled=True)
    hidden = x_full.astype(jnp.float32)
    for layer in range(LAYERS):
        hb = hidden.astype(jnp.bfloat16)
        rim = passed_along(hb[:, width - D_MAX :], "tm", 1)
        extended = jnp.concatenate([rim, hb], axis=1)
        past = lax.dynamic_slice_in_dim(extended, D_MAX - dilations[layer], width, 1)
        hidden = conv_layer(hidden, hb, past, conv_w[layer], conv_b[layer])
    target = lax.dynamic_slice_in_dim(hidden, lax.axis_index("series") * rank_part, rank_part, 0)
    basis_new = basis - 0.5 * (grad_x + (basis - target))
    return (factors_new, m_new, v_new, basis_new)


def solution(mesh):
    return jax.shard_map(
        on_device,
        mesh=mesh,
        in_specs=(
            P("series", "tm"),
            P("series", "tm"),
            P(("series", "tm"), None),
            P(("series", "tm"), None),
            P(("series", "tm"), None),
            P("series", "tm"),
            P(),
            P(),
            P(),
        ),
        out_specs=(
            P(("series", "tm"), None),
            P(("series", "tm"), None),
            P(("series", "tm"), None),
            P("series", "tm"),
        ),
        check_vma=False,
    )
```

profile of v0, /device:TPU:6, one launch (start us, length us, event | category | flops | bytes accessed | tf_op | source)
XLA Modules:
  0.0 517.4 jit_solution(5125097129864647785)
XLA Ops:
  7.2 1.4 convert_element_type.30
  8.7 0.7 convert_element_type.28
  9.4 0.8 convert_element_type.31
  10.2 43.9 %all_gather.7 = bf16[128,512]{1,0:T(8,128)(2,1)S(1)} all-gather(bf16[16,512]{1,0:T(8,128)(2,1)S(1)} %convert_element_type.31), channel_id=1, replica_groups=mesh['series'=8,'tm'=64] {'series'}, dimensions={0}, use_global_device_ids=true | all-gather | bytes 147456 | tf_op jit(solution)/shard_map/all_gather | solution.py:49
  54.1 76.9 %all-gather.2.cloned.1.call-done = bf16[4096,128]{1,0:T(8,128)(2,1)} async-done(((bf16[64,128]{1,0:T(8,128)(2,1)}), bf16[4096,128]{1,0:T(8,128)(2,1)}) %all-gather.2.cloned.1.call-update) | async-done | bytes 1048592 | tf_op jit(solution)/shard_map/all_gather | solution.py:48
  131.0 1.1 broadcast_in_dim.2
  132.2 1.0 copy-done.1
  133.5 1.2 fusion
  134.8 1.9 copy-done
  136.7 1.3 fusion.18
  138.0 0.8 copy.32
  138.9 4.8 fusion.1
  143.9 2.1 collective-permute-start
  152.7 3.1 collective-permute-start.1
  156.0 0.6 collective-permute-done.1
  156.8 2.2 collective-permute-start.2
  159.3 0.6 collective-permute-done.2
  160.1 4.0 collective-permute-start.3
  164.3 0.6 collective-permute-done.3
  165.1 60.5 %reduce-scatter.7.cloned.1.call-done = f32[16,512]{1,0:T(8,128)} async-done(((f32[128,512]{1,0:T(8,128)}), f32[16,512]{1,0:T(8,128)}) %reduce-scatter.7.cloned.1.call-update) | async-done | bytes 32784
  225.6 0.9 copy.33
  226.7 0.7 copy.28
  227.4 282.0 %reduce-scatter.5.cloned.1.call-done = f32[64,128]{1,0:T(8,128)} async-done(((f32[4096,128]{1,0:T(8,128)}), f32[64,128]{1,0:T(8,128)}) %reduce-scatter.5.cloned.1.call-update) | async-done | bytes 32784 | tf_op jit(solution)/shard_map/reduce_scatter | solution.py:55
  509.4 1.4 divide_subtract_fusion
  (43 shorter events, 3.5 us)
Async XLA Ops:
  7.2 123.9 %all-gather.2.cloned.1.call-start = ((), (), s32[]{:S(2)}) async-start(), calls=%async_computation.2 | async-start | bytes 1064960 | tf_op jit(solution)/shard_map/all_gather | solution.py:48
  8.6 217.0 %reduce-scatter.7.cloned.1.call-start = ((), (), s32[]{:S(2)}) async-start(), calls=%async_computation.4 | async-start | bytes 294912
  131.0 2.2 copy-start.1
  131.0 2.5 copy-start.2
  134.8 1.9 copy-start
  138.8 7.2 %copy-start.9 = (f32[4,128]{1,0:T(4,128)S(1)}, f32[4,128]{1,0:T(4,128)}, u32[]{:S(2)}) copy-start(f32[4,128]{1,0:T(4,128)} %param.17) | copy-start | bytes 6148
  138.9 7.2 %copy-start.3 = (bf16[4,2,128,128]{3,2,1,0:T(8,128)(2,1)S(1)}, bf16[4,2,128,128]{3,2,1,0:T(8,128)(2,1)}, u32[]{:S(2)}) copy-start(bf16[4,2,128,128]{3,2,1,0:T(8,128)(2,1)} %param.16) | copy-start | bytes 786436
  138.9 7.4 %copy-start.8 = (s32[4]{0:T(128)S(1)}, s32[4]{0:T(128)}, u32[]{:S(2)}) copy-start(s32[4]{0:T(128)} %param.15) | copy-start | bytes 52
  138.9 8.0 %copy-start.4 = (f32[16,512]{1,0:T(8,128)S(1)}, f32[16,512]{1,0:T(8,128)}, u32[]{:S(2)}) copy-start(f32[16,512]{1,0:T(8,128)} %param.14) | copy-start | bytes 98308
  138.9 370.5 %reduce-scatter.5.cloned.1.call-start = ((), (), s32[]{:S(2)}) async-start(), calls=%async_computation.3 | async-start | bytes 2129920 | tf_op jit(solution)/shard_map/reduce_scatter | solution.py:55
  143.8 365.6 %copy-start.5 = (f32[64,128]{1,0:T(8,128)S(1)}, f32[64,128]{1,0:T(8,128)}, u32[]{:S(2)}) copy-start(f32[64,128]{1,0:T(8,128)} %param.11) | copy-start | bytes 98308
  143.8 365.6 %copy-start.6 = (f32[64,128]{1,0:T(8,128)S(1)}, f32[64,128]{1,0:T(8,128)}, u32[]{:S(2)}) copy-start(f32[64,128]{1,0:T(8,128)} %param.12) | copy-start | bytes 98308
  143.8 365.6 %copy-start.7 = (f32[64,128]{1,0:T(8,128)S(1)}, f32[64,128]{1,0:T(8,128)}, u32[]{:S(2)}) copy-start(f32[64,128]{1,0:T(8,128)} %param.13) | copy-start | bytes 98308
  143.9 8.5 %collective-permute-start = (bf16[128,32]{1,0:T(8,128)(2,1)S(1)}, bf16[128,32]{1,0:T(8,128)(2,1)S(1)}, u32[]{:S(2)}, u32[]{:S(2)}) collective-permute-start(bf16[128,32]{1,0:T(8,128)(2,1)S(1)} %slice.100), channel_id=1, source_target_pairs={{0,1},{1,2},{2,3},{3,4},{4,5},{5,6},{6,7},{7,8},{8,9},{9,10},{10,1... | collective-permute-start | bytes 24584 | tf_op jit(solution)/shard_map/ppermute | solution.py:16
  152.7 3.9 collective-permute-start.1
  156.8 3.1 collective-permute-start.2
  160.1 4.8 collective-permute-start.3
Sparse Core Ops, SparseCore 0:
  10.7 120.2 all-gather.1
  139.0 86.6 reduce-scatter.6
  228.6 280.7 reduce-scatter.4
where the time goes:
time: 518 us; the launch traced here: 517 us
  waiting for transfers between devices  421 us (81%)
  blocking collectives  43.9 us (8%)
  between operations  19.2 us (4%)
  starting transfers between devices  11.6 us (2%)
  matrix products  9.04 us (2%)
  local copies, waits for them, and re-layouts  7.91 us (2%)
    reduce_scatter x1, waiting for transfers between devices, on_device(): lax.psum_scatter(-lax.dot_general(rb, x_full, contract_time, preferred_el...  282 us
    all_gather x1, waiting for transfers between devices, on_device(): lax.all_gather(factors.astype(jnp.bfloat16), 'tm', axis=0, tiled=True)  76.9 us
    unnamed x4, waiting for transfers between devices  60.5 us
    all_gather x1, blocking collectives, on_device(): lax.all_gather(basis.astype(jnp.bfloat16), 'series', axis=0, tiled=True)  43.9 us
    ppermute x4, starting transfers between devices, passed_along(): lax.ppermute(value, axis, [(source, source + steps) for source in range(l...  11.4 us
  transfers between devices with their start and end apart: 7, of which 6 were waited for; matrix products, arithmetic and copies ran while one was open for 2% of the time, Pallas kernels for 0%

commit v1 on v0

--- a/solution.py
+++ b/solution.py
@@ -45,7 +45,10 @@
     rank_part = basis.shape[0]
     total_time = width * lax.axis_size("tm")
     total_series = own_rows * lax.axis_size("tm") * lax.axis_size("series")
-    f_block = lax.all_gather(factors.astype(jnp.bfloat16), "tm", axis=0, tiled=True)
+    f_block = jnp.concatenate(
+        lax.all_to_all(jnp.stack([factors.astype(jnp.bfloat16)] * lax.axis_size("tm")), "tm", 0, 0),
+        axis=0,
+    )
     x_full = lax.all_gather(basis.astype(jnp.bfloat16), "series", axis=0, tiled=True)
     pred = jnp.dot(f_block, x_full, preferred_element_type=jnp.float32)
     resid = expand(tile_mask, TILE) * (y_obs.astype(jnp.float32) - pred)

time: 518 us -> 465 us (0.90)
  waiting for transfers between devices: 421 us -> 348 us
  starting transfers between devices: 11.6 us -> 21.5 us
  blocking collectives: 43.9 us -> 53 us
    all_gather x1 -> x0, waiting for transfers between devices: 76.9 us -> none  [on_device(): lax.all_gather(factors.astype(jnp.bfloat16), 'tm', axis=0, tiled=True)]
    all_to_all x0 -> x1, starting transfers between devices: none -> 14.4 us  [on_device(): lax.all_to_all(jnp.stack([factors.astype(jnp.bfloat16)] * lax.axis_size('...]
    all_gather x1, blocking collectives: 43.9 us -> 53 us  [on_device(): lax.all_gather(basis.astype(jnp.bfloat16), 'series', axis=0, tiled=True)]
    unnamed x4 -> x3, waiting for transfers between devices: 60.5 us -> 64.6 us
  transfers between devices with their start and end apart: 7 -> 7, of which waited for: 6 -> 5; matrix products, arithmetic and copies ran while one was open for 2% -> 2% of each run, Pallas kernels for 0% -> 0%
where the time goes in v1:
time: 465 us; the launch traced here: 464 us
  waiting for transfers between devices  348 us (75%)
  blocking collectives  53 us (11%)
  starting transfers between devices  21.5 us (5%)
  between operations  19.5 us (4%)
  matrix products  9.08 us (2%)
  local copies, waits for them, and re-layouts  8.87 us (2%)
    reduce_scatter x1, waiting for transfers between devices, on_device(): lax.psum_scatter(-lax.dot_general(rb, x_full, contract_time, preferred_el...  282 us
    unnamed x3, waiting for transfers between devices  64.6 us
    all_gather x1, blocking collectives, on_device(): lax.all_gather(basis.astype(jnp.bfloat16), 'series', axis=0, tiled=True)  53 us
    all_to_all x1, starting transfers between devices, on_device(): lax.all_to_all(jnp.stack([factors.astype(jnp.bfloat16)] * lax.axis_size('...  14.4 us
  transfers between devices with their start and end apart: 7, of which 5 were waited for; matrix products, arithmetic and copies ran while one was open for 2% of the time, Pallas kernels for 0%

profile of v1, /device:TPU:6, one launch (start us, length us, event | category | flops | bytes accessed | tf_op | source)
XLA Modules:
  0.0 463.9 jit_solution(7413537225429268687)
XLA Ops:
  7.2 0.8 convert_element_type.30
  7.9 1.2 stack.2
  9.2 14.4 %all-to-all-start = ((bf16[64,64,128]{2,1,0:T(8,128)(2,1)}), bf16[64,64,128]{2,1,0:T(8,128)(2,1)S(1)}, u32[]{:S(2)}, u32[]{:S(2)}) async-start(bf16[64,64,128]{2,1,0:T(8,128)(2,1)} %stack.2), calls=%async_computation | async-start | bytes 2097152 | tf_op jit(solution)/shard_map/all_to_all | solution.py:49
  23.6 0.7 convert_element_type.28
  24.4 0.8 convert_element_type.31
  25.1 53.0 %all_gather.3 = bf16[128,512]{1,0:T(8,128)(2,1)S(1)} all-gather(bf16[16,512]{1,0:T(8,128)(2,1)S(1)} %convert_element_type.31), channel_id=1, replica_groups=mesh['series'=8,'tm'=64] {'series'}, dimensions={0}, use_global_device_ids=true | all-gather | bytes 147456 | tf_op jit(solution)/shard_map/all_gather | solution.py:52
  78.1 1.1 broadcast_in_dim.2
  79.3 1.0 copy-done.1
  80.3 1.2 fusion
  81.6 1.9 copy-done
  83.5 1.3 fusion.18
  84.8 0.8 copy.32
  85.8 4.8 %fusion.1 = f32[4096,128]{1,0:T(8,128)} fusion(bf16[4096,512]{1,0:T(8,128)(2,1)} %copy-done, bf16[128,512]{1,0:T(8,128)(2,1)S(1)} %all_gather.3), kind=kOutput, calls=%fused_computation.3 | convolution fusion | flops 537919488 | bytes 6422528 | tf_op jit(solution)/shard_map/dot_general | solution.py:59
  90.8 1.3 collective-permute-start
  98.8 1.3 collective-permute-start.1
  100.2 0.6 collective-permute-done.1
  101.1 2.2 collective-permute-start.2
  103.5 0.6 collective-permute-done.2
  104.4 2.2 collective-permute-start.3
  107.7 64.5 %reduce-scatter.7.cloned.1.call-done = f32[16,512]{1,0:T(8,128)} async-done(((f32[128,512]{1,0:T(8,128)}), f32[16,512]{1,0:T(8,128)}) %reduce-scatter.7.cloned.1.call-update) | async-done | bytes 32784
  172.2 0.9 copy.33
  173.3 0.7 copy.28
  174.0 281.6 %reduce-scatter.5.cloned.1.call-done = f32[64,128]{1,0:T(8,128)} async-done(((f32[4096,128]{1,0:T(8,128)}), f32[64,128]{1,0:T(8,128)}) %reduce-scatter.5.cloned.1.call-update) | async-done | bytes 32784 | tf_op jit(solution)/shard_map/reduce_scatter | solution.py:58
  455.6 1.4 divide_subtract_fusion
  (41 shorter events, 3.7 us)
Async XLA Ops:
  9.2 69.0 %all-to-all-start = ((bf16[64,64,128]{2,1,0:T(8,128)(2,1)}), bf16[64,64,128]{2,1,0:T(8,128)(2,1)S(1)}, u32[]{:S(2)}, u32[]{:S(2)}) async-start(bf16[64,64,128]{2,1,0:T(8,128)(2,1)} %stack.2), calls=%async_computation | async-start | bytes 2097152 | tf_op jit(solution)/shard_map/all_to_all | solution.py:49
  23.5 148.6 %reduce-scatter.7.cloned.1.call-start = ((), (), s32[]{:S(2)}) async-start(), calls=%async_computation.4 | async-start | bytes 294912
  78.1 2.2 copy-start.1
  81.6 1.9 copy-start
  85.7 6.4 %copy-start.8 = (f32[4,128]{1,0:T(4,128)S(1)}, f32[4,128]{1,0:T(4,128)}, u32[]{:S(2)}) copy-start(f32[4,128]{1,0:T(4,128)} %param.17) | copy-start | bytes 6148
  85.7 6.4 %copy-start.2 = (bf16[4,2,128,128]{3,2,1,0:T(8,128)(2,1)S(1)}, bf16[4,2,128,128]{3,2,1,0:T(8,128)(2,1)}, u32[]{:S(2)}) copy-start(bf16[4,2,128,128]{3,2,1,0:T(8,128)(2,1)} %param.16) | copy-start | bytes 786436
  85.7 6.6 %copy-start.7 = (s32[4]{0:T(128)S(1)}, s32[4]{0:T(128)}, u32[]{:S(2)}) copy-start(s32[4]{0:T(128)} %param.15) | copy-start | bytes 52
  85.7 7.2 %copy-start.3 = (f32[16,512]{1,0:T(8,128)S(1)}, f32[16,512]{1,0:T(8,128)}, u32[]{:S(2)}) copy-start(f32[16,512]{1,0:T(8,128)} %param.14) | copy-start | bytes 98308
  85.8 369.8 %reduce-scatter.5.cloned.1.call-start = ((), (), s32[]{:S(2)}) async-start(), calls=%async_computation.3 | async-start | bytes 2129920 | tf_op jit(solution)/shard_map/reduce_scatter | solution.py:58
  90.7 365.0 %copy-start.4 = (f32[64,128]{1,0:T(8,128)S(1)}, f32[64,128]{1,0:T(8,128)}, u32[]{:S(2)}) copy-start(f32[64,128]{1,0:T(8,128)} %param.11) | copy-start | bytes 98308
  90.7 364.9 %copy-start.5 = (f32[64,128]{1,0:T(8,128)S(1)}, f32[64,128]{1,0:T(8,128)}, u32[]{:S(2)}) copy-start(f32[64,128]{1,0:T(8,128)} %param.12) | copy-start | bytes 98308
  90.7 364.9 %copy-start.6 = (f32[64,128]{1,0:T(8,128)S(1)}, f32[64,128]{1,0:T(8,128)}, u32[]{:S(2)}) copy-start(f32[64,128]{1,0:T(8,128)} %param.13) | copy-start | bytes 98308
  90.8 7.6 %collective-permute-start = (bf16[128,32]{1,0:T(8,128)(2,1)S(1)}, bf16[128,32]{1,0:T(8,128)(2,1)S(1)}, u32[]{:S(2)}, u32[]{:S(2)}) collective-permute-start(bf16[128,32]{1,0:T(8,128)(2,1)S(1)} %slice.100), channel_id=1, source_target_pairs={{0,1},{1,2},{2,3},{3,4},{4,5},{5,6},{6,7},{7,8},{8,9},{9,10},{10,1... | collective-permute-start | bytes 24584 | tf_op jit(solution)/shard_map/ppermute | solution.py:16
  98.8 2.1 collective-permute-start.1
  101.1 3.1 collective-permute-start.2
  104.4 3.1 collective-permute-start.3
Sparse Core Ops, SparseCore 0:
  85.8 86.3 reduce-scatter.6
  175.2 280.3 reduce-scatter.4
